TPU v7x, 128 devices: a whole 4x4x4 slice. The times are simulated.
128 devices in a mesh: seq: 16 (over y, x), expert: 4 (over z), mp: 2 (over core).
Axes of the slice: x: 4, y: 4, z: 4, core: 2. Of those that a mesh axis runs over, the one named last changes fastest.
Arguments:
- activations: bfloat16 [16384, 4096], P('seq', ('expert', 'mp')), may hold values from -6 to 6
- output_gradient: bfloat16 [16384, 4096], P('seq', ('expert', 'mp')), may hold values from -1.5 to 1.5
- input_state_map: bfloat16 [16384, 16], P('seq'), may hold values from -3 to 3
- output_state_map: bfloat16 [16384, 16], P('seq'), may hold values from -3 to 3
- head_decay_speed: float32 [64], P(('expert', 'mp')), may hold values from 3.0517578e-06 to 0.05, as said below
- spike_decay_level: int32 [16384], P('seq'), may hold values from 0 to 2, as said below
- assign: int32 [128], replicated, may hold values from 0 to 15, as said below
- expert_up_weight: bfloat16 [4, 4096, 12288], P('expert', 'mp', 'seq'), may hold values from -0.09375 to 0.09375
- expert_down_weight: bfloat16 [4, 12288, 4096], P('expert', 'seq', 'mp'), may hold values from -0.0546875 to 0.0546875
Outputs:
- grad_x: float32 [16384, 4096], P('seq', ('expert', 'mp'))
- grad_w_up: float32 [4, 4096, 12288], P('expert', 'mp', 'seq')
- grad_w_down: float32 [4, 12288, 4096], P('expert', 'seq', 'mp')
Inputs may be any that keep to these rules, and one draw needn't show every extreme that they name: `head_decay_speed`: some of the heads keep a tenth or more of their state over the whole sequence, the others lose it within some tens of tokens. `spike_decay_level`: at most three tokens of the sequence have a nonzero level. `assign`: numbers below 4 are the window's experts: the 8 blocks of one index of seq hold at most one block of each of them, each takes at most 8 blocks in all, and one takes exactly 8.
All inputs are finite; a program needn't handle non-finite values.
Results may differ from a plain program's by a relative error of at most 0.019.
Values may be sent and summed in bfloat16 or wider, within the bound.
No kernel may reach another device: no remote copies, remote signals or barrier semaphores. Data moves between devices by JAX's collectives and lax.ppermute only.
A program may use at most 128 MiB of HBM per device.

v0:
```python
import jax
import jax.numpy as jnp
from jax import lax
from jax.sharding import PartitionSpec as P

HEAD = 64
STATE = 16
BLOCK = 128
spike_position_step = 0.3
highest = lax.Precision.HIGHEST


def from_behind(value, axis, steps):
    count = lax.axis_size(axis)
    first, last = (max(0, -steps), min(count, count - steps))
    return lax.ppermute(value, axis, [(source, source + steps) for source in range(first, last)])


def rounded(rounded_in):
    return lax.optimization_barrier(rounded_in.astype(jnp.bfloat16)).astype(jnp.float32)


def split_parts(values):
    high_part = values.astype(jnp.bfloat16)
    low_part = (values - high_part.astype(jnp.float32)).astype(jnp.bfloat16)
    return (high_part, low_part)


def mixing(cum_block, scores, causal):
    spread = cum_block.T[:, :, None] - cum_block.T[:, None, :]
    spread = jnp.where(causal[None], spread, -jnp.inf)
    return jnp.exp(spread) * scores[None]


def narrow(gathered, exp_index, mp_index, half_width):
    row_set = lax.dynamic_index_in_dim(gathered, exp_index, 0, keepdims=False)
    return lax.dynamic_slice_in_dim(row_set, mp_index * half_width, half_width, 1)


def compact(select, gathered, half_width):
    shaped = gathered.reshape(select.shape[1], -1, half_width)
    rows_out = jnp.einsum("js,srf->jrf", select, shaped, preferred_element_type=jnp.float32)
    return rows_out.astype(jnp.bfloat16).reshape(-1, half_width)


def per_device(
    activations,
    output_gradient,
    input_state_map,
    output_state_map,
    head_decay_speed,
    spike_decay_level,
    assign,
    expert_up_weight,
    expert_down_weight,
):
    tokens, slice_width = activations.shape
    heads_dev = slice_width // HEAD
    seq_count = lax.axis_size("seq")
    exp_count = lax.axis_size("expert")
    mp_count = lax.axis_size("mp")
    seq_index = lax.axis_index("seq")
    exp_index = lax.axis_index("expert")
    mp_index = lax.axis_index("mp")
    my_slice = exp_index * mp_count + mp_index
    slice_half = my_slice // exp_count
    half_width = slice_width * exp_count
    slot_total = seq_count // 2
    input_scale = jnp.sqrt(1.0 - jnp.exp(-2.0 * head_decay_speed))
    cum_level = jnp.cumsum(
        -head_decay_speed[None, :]
        - spike_position_step * spike_decay_level.astype(jnp.float32)[:, None],
        axis=0,
    )
    b_float = input_state_map.astype(jnp.float32)
    c_float = output_state_map.astype(jnp.float32)
    act_heads = activations.reshape(tokens, heads_dev, HEAD)
    scaled = act_heads.astype(jnp.float32) * input_scale[None, :, None]
    span_rows = min(512, tokens)
    span_count = tokens // span_rows
    causal = jnp.arange(span_rows)[:, None] >= jnp.arange(span_rows)[None, :]
    zero_level = jnp.zeros((heads_dev,), jnp.float32)
    carry_state = jnp.zeros((heads_dev, HEAD, STATE), jnp.float32)
    pieces = []
    for position in range(span_count):
        first_row = position * span_rows
        last_row = first_row + span_rows
        cum_block = cum_level[first_row:last_row]
        start_level = cum_level[first_row - 1] if position > 0 else zero_level
        scores = jnp.dot(
            output_state_map[first_row:last_row],
            input_state_map[first_row:last_row].T,
            preferred_element_type=jnp.float32,
        )
        weights = mixing(cum_block, scores, causal)
        weight_high, weight_low = split_parts(weights)
        x_span = act_heads[first_row:last_row]
        inner_part = jnp.einsum(
            "hts,shp->thp", weight_high, x_span, preferred_element_type=jnp.float32
        )
        inner_part = inner_part + jnp.einsum(
            "hts,shp->thp", weight_low, x_span, preferred_element_type=jnp.float32
        )
        inner_part = inner_part * input_scale[None, :, None]
        carried = jnp.exp(cum_block - start_level[None, :])[:, :, None] * jnp.einsum(
            "tn,hpn->thp", c_float[first_row:last_row], carry_state, precision=highest
        )
        pieces.append(inner_part + carried)
        end_level = cum_block[-1]
        tail_decay = jnp.exp(end_level[None, :] - cum_block)
        carry_state = jnp.exp(end_level - start_level)[:, None, None] * carry_state + jnp.einsum(
            "shp,sn->hpn",
            scaled[first_row:last_row] * tail_decay[:, :, None],
            b_float[first_row:last_row],
            precision=highest,
        )
    device_decay = jnp.exp(cum_level[-1])
    flat_state = carry_state.reshape(heads_dev, HEAD * STATE)

    def relay_state(rounds, carried_in):
        return from_behind(
            (device_decay[:, None] * carried_in + flat_state).astype(jnp.bfloat16), "seq", 1
        ).astype(jnp.float32)

    incoming = lax.fori_loop(0, seq_count - 1, relay_state, jnp.zeros_like(flat_state))
    incoming = incoming.reshape(heads_dev, HEAD, STATE)
    outputs = jnp.concatenate(pieces, axis=0) + jnp.exp(cum_level)[:, :, None] * jnp.einsum(
        "tn,hpn->thp", c_float, incoming, precision=highest
    )
    mixed_out = (activations.astype(jnp.float32) + outputs.reshape(tokens, slice_width)).astype(
        jnp.bfloat16
    )
    blocks_dev = tokens // BLOCK
    route_table = assign.reshape(seq_count, blocks_dev)
    own_row = lax.dynamic_index_in_dim(route_table, seq_index, 0, keepdims=False)
    chosen = (own_row[None, :] == jnp.arange(exp_count)[:, None]).astype(jnp.bfloat16)
    h_pick = jnp.einsum(
        "eb,brf->erf",
        chosen,
        mixed_out.reshape(blocks_dev, BLOCK, slice_width),
        preferred_element_type=jnp.float32,
    ).astype(jnp.bfloat16)
    g_pick = jnp.einsum(
        "eb,brf->erf",
        chosen,
        output_gradient.reshape(blocks_dev, BLOCK, slice_width),
        preferred_element_type=jnp.float32,
    ).astype(jnp.bfloat16)
    h_full, g_full = (
        lax.all_gather(h_pick, ("expert", "mp"), axis=2, tiled=True),
        lax.all_gather(g_pick, ("expert", "mp"), axis=2, tiled=True),
    )
    h_block = narrow(h_full, exp_index, mp_index, half_width)
    g_block = narrow(g_full, exp_index, mp_index, half_width)
    h_all, g_all = (
        lax.all_gather(h_block, "seq", axis=0, tiled=True),
        lax.all_gather(g_block, "seq", axis=0, tiled=True),
    )
    present = jnp.any(route_table == exp_index, axis=1)
    slot_of = jnp.cumsum(present.astype(jnp.int32)) - 1
    select = ((slot_of[None, :] == jnp.arange(slot_total)[:, None]) & present[None, :]).astype(
        jnp.bfloat16
    )
    x_rows = compact(select, h_all, half_width)
    g_rows = compact(select, g_all, half_width)
    up_local = expert_up_weight[0]
    down_local = expert_down_weight[0]
    pre_act = lax.psum(
        rounded(jnp.dot(x_rows, up_local, preferred_element_type=jnp.float32)).astype(jnp.bfloat16),
        "mp",
    ).astype(jnp.float32)
    activation = jax.nn.silu(pre_act).astype(jnp.bfloat16)
    down_grad = jnp.einsum("tf,td->fd", activation, g_rows, preferred_element_type=jnp.float32)
    act_grad = lax.psum(
        rounded(
            jnp.einsum("td,fd->tf", g_rows, down_local, preferred_element_type=jnp.float32)
        ).astype(jnp.bfloat16),
        "mp",
    ).astype(jnp.float32)
    sigmoid_pre = jax.nn.sigmoid(pre_act)
    pre_grad = (act_grad * sigmoid_pre * (1.0 + pre_act * (1.0 - sigmoid_pre))).astype(jnp.bfloat16)
    up_grad = jnp.einsum("td,tf->df", x_rows, pre_grad, preferred_element_type=jnp.float32)
    row_grad = jnp.einsum("tf,df->td", pre_grad, up_local, preferred_element_type=jnp.float32)
    row_grad = row_grad.astype(jnp.bfloat16).reshape(slot_total, BLOCK, half_width)
    spread_rows = jnp.einsum("js,jrf->srf", select, row_grad, preferred_element_type=jnp.float32)
    back_rows = lax.psum_scatter(
        spread_rows.reshape(BLOCK * lax.axis_size("seq"), half_width).astype(jnp.bfloat16),
        "seq",
        scatter_dimension=0,
        tiled=True,
    )
    arrived = lax.all_gather(back_rows[None], ("expert", "mp"), axis=0, tiled=True)
    halves = lax.dynamic_index_in_dim(
        arrived.reshape(exp_count, mp_count, BLOCK, half_width), slice_half, 1, keepdims=False
    )
    returned = lax.dynamic_slice_in_dim(halves, my_slice % exp_count * slice_width, slice_width, 2)
    token_grad = jnp.einsum("eb,erf->brf", chosen, returned, preferred_element_type=jnp.float32)
    total_grad = output_gradient.astype(jnp.float32) + token_grad.reshape(tokens, slice_width)
    grad_view = total_grad.reshape(tokens, heads_dev, HEAD)
    adjoint = jnp.zeros((heads_dev, HEAD, STATE), jnp.float32)
    back_pieces = [None] * span_count
    for position in reversed(range(span_count)):
        first_row = position * span_rows
        last_row = first_row + span_rows
        cum_block = cum_level[first_row:last_row]
        start_level = cum_level[first_row - 1] if position > 0 else zero_level
        scores = jnp.dot(
            output_state_map[first_row:last_row],
            input_state_map[first_row:last_row].T,
            preferred_element_type=jnp.float32,
        )
        weights = mixing(cum_block, scores, causal)
        weight_high, weight_low = split_parts(weights)
        grad_high, grad_low = split_parts(grad_view[first_row:last_row])
        inner_part = jnp.einsum(
            "hts,thp->shp", weight_high, grad_high, preferred_element_type=jnp.float32
        )
        inner_part = inner_part + jnp.einsum(
            "hts,thp->shp", weight_high, grad_low, preferred_element_type=jnp.float32
        )
        inner_part = inner_part + jnp.einsum(
            "hts,thp->shp", weight_low, grad_high, preferred_element_type=jnp.float32
        )
        end_level = cum_block[-1]
        tail_decay = jnp.exp(end_level[None, :] - cum_block)
        carried = tail_decay[:, :, None] * jnp.einsum(
            "sn,hpn->shp", b_float[first_row:last_row], adjoint, precision=highest
        )
        back_pieces[position] = inner_part + carried
        lead_decay = jnp.exp(cum_block - start_level[None, :])
        adjoint = jnp.exp(end_level - start_level)[:, None, None] * adjoint + jnp.einsum(
            "rhp,rn->hpn",
            grad_view[first_row:last_row] * lead_decay[:, :, None],
            c_float[first_row:last_row],
            precision=highest,
        )
    flat_adjoint = adjoint.reshape(heads_dev, HEAD * STATE)

    def relay_adjoint(rounds, carried_in):
        return from_behind(
            (device_decay[:, None] * carried_in + flat_adjoint).astype(jnp.bfloat16), "seq", -1
        ).astype(jnp.float32)

    later_adjoint = lax.fori_loop(0, seq_count - 1, relay_adjoint, jnp.zeros_like(flat_adjoint))
    later_adjoint = later_adjoint.reshape(heads_dev, HEAD, STATE)
    scan_grad = jnp.concatenate(back_pieces, axis=0) + jnp.exp(cum_level[-1][None, :] - cum_level)[
        :, :, None
    ] * jnp.einsum("sn,hpn->shp", b_float, later_adjoint, precision=highest)
    grad_x = total_grad + (input_scale[None, :, None] * scan_grad).reshape(tokens, slice_width)
    return (grad_x, up_grad[None], down_grad[None])


def solution(mesh):
    in_specs = (
        P("seq", ("expert", "mp")),
        P("seq", ("expert", "mp")),
        P("seq", None),
        P("seq", None),
        P(("expert", "mp")),
        P("seq"),
        P(),
        P("expert", "mp", "seq"),
        P("expert", "seq", "mp"),
    )
    out_specs = (P("seq", ("expert", "mp")), P("expert", "mp", "seq"), P("expert", "seq", "mp"))
    return jax.shard_map(
        per_device, mesh=mesh, in_specs=in_specs, out_specs=out_specs, check_vma=False
    )
```

profile of v0, /device:TPU:6, one launch (start us, length us, event | category | flops | bytes accessed | tf_op | source)
XLA Modules:
  0.0 771.0 jit_solution(8821121066339142544)
XLA Ops:
  23.1 4.1 fusion.62
  47.4 123.4 %while.22 = (s32[]{:T(128)}, f32[8,1024]{1,0:T(8,128)S(1)}, f32[8]{0:T(128)}, f32[8,1024]{1,0:T(8,128)S(1)}, s32[]{:T(128)}, /*index=5*/s32[]{:T(128)}) while((s32[]{:T(128)}, f32[8,1024]{1,0:T(8,128)S(1)}, f32[8]{0:T(128)}, f32[8,1024]{1,0:T(8,128)S(1)}, s32[]{:T(128)}, /*index=5*/s32[]{:T(128)}) %tuple.59), condition=%wide.region_6.7_spmd.clone, body=%wide.region_5.6_spmd.clone.sunk | while | flops 40963 | bytes 196759 | solution.py:125
  54.5 5.5 collective-permute-start
  62.1 6.3 collective-permute-start
  70.5 6.3 collective-permute-start
  78.9 6.3 collective-permute-start
  87.3 6.3 collective-permute-start
  95.7 6.3 collective-permute-start
  104.2 6.3 collective-permute-start
  112.6 6.3 collective-permute-start
  121.0 6.3 collective-permute-start
  129.4 6.3 collective-permute-start
  137.8 6.3 collective-permute-start
  146.2 6.3 collective-permute-start
  154.7 6.3 collective-permute-start
  163.1 6.3 collective-permute-start
  189.0 35.8 %all-gather.11.cloned.1.call-done = bf16[4,128,4096]{2,0,1:T(4,128)(2,1)} async-done(((bf16[4,128,512]{2,0,1:T(4,128)(2,1)}), bf16[4,128,4096]{2,0,1:T(4,128)(2,1)}) %all-gather.11.cloned.1.call-update) | async-done | bytes 4194320 | tf_op jit(solution)/shard_map/all_gather | solution.py:150
  229.3 34.2 %all-gather.9.cloned.1.call-done = bf16[4,128,4096]{2,0,1:T(4,128)(2,1)} async-done(((bf16[4,128,512]{2,0,1:T(4,128)(2,1)}), bf16[4,128,4096]{2,0,1:T(4,128)(2,1)}) %all-gather.9.cloned.1.call-update) | async-done | bytes 4194320 | tf_op jit(solution)/shard_map/all_gather | solution.py:151
  268.7 69.0 %all-gather.15.cloned.1.call-done = bf16[1,2048,2048]{2,1,0:T(8,128)(2,1)} async-done(((bf16[1,128,2048]{2,1,0:T(8,128)(2,1)}), bf16[1,2048,2048]{2,1,0:T(8,128)(2,1)}) %all-gather.15.cloned.1.call-update) | async-done | bytes 8388624 | tf_op jit(solution)/shard_map/all_gather | solution.py:156
  337.7 12.5 %fusion.56 = bf16[8,128,2048]{2,0,1:T(8,128)(2,1)S(1)} fusion(bf16[16,128,2048]{2,1,0:T(8,128)(2,1)} %bitcast.153, s32[16]{0:T(128)S(1)} %add_reduce_fusion, pred[16]{0:T(512)(128)(4,1)S(1)} %compare_reduce_fusion), kind=kOutput, calls=%fused_computation.58 | convolution fusion | flops 69206272 | bytes 12582992 | tf_op jit(solution)/shard_map/js,srf->jrf/dot_general | solution.py:42
  355.0 4.5 fusion.79
  359.5 51.2 %all-gather.13.cloned.1.call-done = bf16[1,2048,2048]{2,1,0:T(8,128)(2,1)} async-done(((bf16[1,128,2048]{2,1,0:T(8,128)(2,1)}), bf16[1,2048,2048]{2,1,0:T(8,128)(2,1)}) %all-gather.13.cloned.1.call-update) | async-done | bytes 8388624 | tf_op jit(solution)/shard_map/all_gather | solution.py:157
  410.7 12.5 %fusion.53 = bf16[8,128,2048]{2,0,1:T(8,128)(2,1)S(1)} fusion(bf16[16,128,2048]{2,1,0:T(8,128)(2,1)} %bitcast.154, s32[16]{0:T(128)S(1)} %add_reduce_fusion, pred[16]{0:T(512)(128)(4,1)S(1)} %compare_reduce_fusion), kind=kOutput, calls=%fused_computation.57 | convolution fusion | flops 69206272 | bytes 12582992 | tf_op jit(solution)/shard_map/js,srf->jrf/dot_general | solution.py:42
  427.6 4.6 fusion.76
  432.3 28.9 %all-reduce.3.cloned.1.call-done = (bf16[1024,768]{1,0:T(8,128)(2,1)}, bf16[1024,768]{1,0:T(8,128)(2,1)}) async-done(((bf16[1024,768]{1,0:T(8,128)(2,1)}, bf16[1024,768]{1,0:T(8,128)(2,1)}), (bf16[1024,768]{1,0:T(8,128)(2,1)}, bf16[1024,768]{1,0:T(8,128)(2,1)})) %all-reduce.3.cloned.1.call-update) | async-done | bytes 3145744 | tf_op jit(solution)/shard_map/psum | solution.py:168
  461.1 6.9 convolution_convert_fusion.1
  468.0 6.9 convolution_convert_fusion
  474.9 11.3 %copy.146 = bf16[16,128,2048]{2,1,0:T(8,128)(2,1)} copy(bf16[16,128,2048]{2,0,1:T(8,128)(2,1)} %convolution_convert_fusion) | data formatting | bytes 16777216 | tf_op jit(solution)/shard_map/convert_element_type | solution.py:187
  486.3 87.0 %reduce-scatter.2.cloned.1.call-done = bf16[128,2048]{1,0:T(8,128)(2,1)} async-done(((bf16[2048,2048]{1,0:T(8,128)(2,1)}), bf16[128,2048]{1,0:T(8,128)(2,1)}) %reduce-scatter.2.cloned.1.call-update) | async-done | bytes 524304 | tf_op jit(solution)/shard_map/reduce_scatter | solution.py:186
  573.4 7.8 %convolution_bitcast_fusion = f32[1,768,2048]{2,1,0:T(8,128)} fusion(bf16[1024,2048]{1,0:T(8,128)(2,1)} %bitcast.163, bf16[1024,768]{1,0:T(8,128)(2,1)S(1)} %copy-done.44), kind=kOutput, calls=%fused_computation.59 | convolution fusion | flops 3225944064 | bytes 12058624 | tf_op jit(solution)/shard_map/tf,td->fd/dot_general | solution.py:173
  581.3 6.1 convolution_bitcast_fusion.1
  587.4 19.6 %all-gather.17.cloned.1.call-done = bf16[1024,2048]{1,0:T(8,128)(2,1)} async-done(((bf16[128,2048]{1,0:T(8,128)(2,1)}), bf16[1024,2048]{1,0:T(8,128)(2,1)}) %all-gather.17.cloned.1.call-update) | async-done | bytes 4194320 | tf_op jit(solution)/shard_map/all_gather | solution.py:192
  636.8 117.3 %while.23 = (s32[]{:T(128)}, f32[8,1024]{1,0:T(8,128)S(1)}, f32[8]{0:T(128)S(1)}, f32[8,1024]{1,0:T(8,128)S(1)}, s32[]{:T(128)}, /*index=5*/s32[]{:T(128)}) while((s32[]{:T(128)}, f32[8,1024]{1,0:T(8,128)S(1)}, f32[8]{0:T(128)S(1)}, f32[8,1024]{1,0:T(8,128)S(1)}, s32[]{:T(128)}, /*index=5*/s32[]{:T(128)}) %tuple.80), condition=%wide.region_10.11_spmd.clone, body=%wide.region_9.10_spmd.clone.sunk | while | flops 40963 | bytes 196759 | solution.py:244
  639.6 5.0 collective-permute-done.1
  646.6 5.8 collective-permute-done.1
  654.4 5.8 collective-permute-done.1
  662.2 5.8 collective-permute-done.1
  670.0 5.8 collective-permute-done.1
  677.9 5.8 collective-permute-done.1
  685.7 5.8 collective-permute-done.1
  693.5 5.8 collective-permute-done.1
  701.3 5.8 collective-permute-done.1
  709.1 5.8 collective-permute-done.1
  716.9 5.8 collective-permute-done.1
  724.7 5.9 collective-permute-done.1
  732.6 5.8 collective-permute-done.1
  740.5 5.8 collective-permute-done.1
  748.3 5.8 collective-permute-done.1
  (272 shorter events, 178.5 us)
Async XLA Ops:
  7.2 347.8 %copy-start = (bf16[1,2048,768]{2,1,0:T(8,128)(2,1)S(1)}, bf16[1,2048,768]{2,1,0:T(8,128)(2,1)}, u32[]{:S(2)}) copy-start(bf16[1,2048,768]{2,1,0:T(8,128)(2,1)} %param.20) | copy-start | bytes 9437188
  7.2 9.9 %copy-start.16 = (bf16[1024,16]{0,1:T(8,128)(2,1)S(1)}, bf16[1024,16]{0,1:T(8,128)(2,1)}, u32[]{:S(2)}) copy-start(bf16[1024,16]{0,1:T(8,128)(2,1)} %param.15) | copy-start | bytes 98308
  7.2 9.9 %copy-start.13 = (bf16[1024,16]{0,1:T(8,128)(2,1)S(1)}, bf16[1024,16]{0,1:T(8,128)(2,1)}, u32[]{:S(2)}) copy-start(bf16[1024,16]{0,1:T(8,128)(2,1)} %param.16) | copy-start | bytes 98308
  7.2 217.5 %all-gather.11.cloned.1.call-start = ((), (), s32[]{:S(2)}) async-start(), calls=%async_computation.2 | async-start | bytes 4718592 | tf_op jit(solution)/shard_map/all_gather | solution.py:150
  7.4 30.9 %copy-start.20 = (pred[512,512]{1,0:T(8,128)(4,1)}, pred[512,512]{1,0:T(8,128)(4,1)S(1)}, u32[]{:S(2)}) copy-start(pred[512,512]{1,0:T(8,128)(4,1)S(1)} %iota_compare_fusion) | copy-start | bytes 786436
  48.1 5.6 collective-permute-start
  54.5 6.9 collective-permute-start
  62.1 7.7 %collective-permute-start = (bf16[8,1024]{1,0:T(8,128)(2,1)S(1)}, bf16[8,1024]{1,0:T(8,128)(2,1)S(1)}, u32[]{:S(2)}, u32[]{:S(2)}) collective-permute-start(bf16[8,1024]{1,0:T(8,128)(2,1)S(1)} %fusion.212), channel_id=1, source_target_pairs={{0,8},{8,16},{16,24},{24,32},{32,40},{40,48},{48,56},{56,64},{64,7... | collective-permute-start | bytes 49160 | tf_op jit(solution)/shard_map/while/body/eval_jaxpr/ppermute | solution.py:16
  70.5 7.7 %collective-permute-start = (bf16[8,1024]{1,0:T(8,128)(2,1)S(1)}, bf16[8,1024]{1,0:T(8,128)(2,1)S(1)}, u32[]{:S(2)}, u32[]{:S(2)}) collective-permute-start(bf16[8,1024]{1,0:T(8,128)(2,1)S(1)} %fusion.212), channel_id=1, source_target_pairs={{0,8},{8,16},{16,24},{24,32},{32,40},{40,48},{48,56},{56,64},{64,7... | collective-permute-start | bytes 49160 | tf_op jit(solution)/shard_map/while/body/eval_jaxpr/ppermute | solution.py:16
  78.9 7.7 %collective-permute-start = (bf16[8,1024]{1,0:T(8,128)(2,1)S(1)}, bf16[8,1024]{1,0:T(8,128)(2,1)S(1)}, u32[]{:S(2)}, u32[]{:S(2)}) collective-permute-start(bf16[8,1024]{1,0:T(8,128)(2,1)S(1)} %fusion.212), channel_id=1, source_target_pairs={{0,8},{8,16},{16,24},{24,32},{32,40},{40,48},{48,56},{56,64},{64,7... | collective-permute-start | bytes 49160 | tf_op jit(solution)/shard_map/while/body/eval_jaxpr/ppermute | solution.py:16
  87.3 7.7 %collective-permute-start = (bf16[8,1024]{1,0:T(8,128)(2,1)S(1)}, bf16[8,1024]{1,0:T(8,128)(2,1)S(1)}, u32[]{:S(2)}, u32[]{:S(2)}) collective-permute-start(bf16[8,1024]{1,0:T(8,128)(2,1)S(1)} %fusion.212), channel_id=1, source_target_pairs={{0,8},{8,16},{16,24},{24,32},{32,40},{40,48},{48,56},{56,64},{64,7... | collective-permute-start | bytes 49160 | tf_op jit(solution)/shard_map/while/body/eval_jaxpr/ppermute | solution.py:16
  95.7 7.7 %collective-permute-start = (bf16[8,1024]{1,0:T(8,128)(2,1)S(1)}, bf16[8,1024]{1,0:T(8,128)(2,1)S(1)}, u32[]{:S(2)}, u32[]{:S(2)}) collective-permute-start(bf16[8,1024]{1,0:T(8,128)(2,1)S(1)} %fusion.212), channel_id=1, source_target_pairs={{0,8},{8,16},{16,24},{24,32},{32,40},{40,48},{48,56},{56,64},{64,7... | collective-permute-start | bytes 49160 | tf_op jit(solution)/shard_map/while/body/eval_jaxpr/ppermute | solution.py:16
  104.2 7.7 %collective-permute-start = (bf16[8,1024]{1,0:T(8,128)(2,1)S(1)}, bf16[8,1024]{1,0:T(8,128)(2,1)S(1)}, u32[]{:S(2)}, u32[]{:S(2)}) collective-permute-start(bf16[8,1024]{1,0:T(8,128)(2,1)S(1)} %fusion.212), channel_id=1, source_target_pairs={{0,8},{8,16},{16,24},{24,32},{32,40},{40,48},{48,56},{56,64},{64,7... | collective-permute-start | bytes 49160 | tf_op jit(solution)/shard_map/while/body/eval_jaxpr/ppermute | solution.py:16
  112.6 7.7 %collective-permute-start = (bf16[8,1024]{1,0:T(8,128)(2,1)S(1)}, bf16[8,1024]{1,0:T(8,128)(2,1)S(1)}, u32[]{:S(2)}, u32[]{:S(2)}) collective-permute-start(bf16[8,1024]{1,0:T(8,128)(2,1)S(1)} %fusion.212), channel_id=1, source_target_pairs={{0,8},{8,16},{16,24},{24,32},{32,40},{40,48},{48,56},{56,64},{64,7... | collective-permute-start | bytes 49160 | tf_op jit(solution)/shard_map/while/body/eval_jaxpr/ppermute | solution.py:16
  121.0 7.7 %collective-permute-start = (bf16[8,1024]{1,0:T(8,128)(2,1)S(1)}, bf16[8,1024]{1,0:T(8,128)(2,1)S(1)}, u32[]{:S(2)}, u32[]{:S(2)}) collective-permute-start(bf16[8,1024]{1,0:T(8,128)(2,1)S(1)} %fusion.212), channel_id=1, source_target_pairs={{0,8},{8,16},{16,24},{24,32},{32,40},{40,48},{48,56},{56,64},{64,7... | collective-permute-start | bytes 49160 | tf_op jit(solution)/shard_map/while/body/eval_jaxpr/ppermute | solution.py:16
  129.4 7.7 %collective-permute-start = (bf16[8,1024]{1,0:T(8,128)(2,1)S(1)}, bf16[8,1024]{1,0:T(8,128)(2,1)S(1)}, u32[]{:S(2)}, u32[]{:S(2)}) collective-permute-start(bf16[8,1024]{1,0:T(8,128)(2,1)S(1)} %fusion.212), channel_id=1, source_target_pairs={{0,8},{8,16},{16,24},{24,32},{32,40},{40,48},{48,56},{56,64},{64,7... | collective-permute-start | bytes 49160 | tf_op jit(solution)/shard_map/while/body/eval_jaxpr/ppermute | solution.py:16
  137.8 7.7 %collective-permute-start = (bf16[8,1024]{1,0:T(8,128)(2,1)S(1)}, bf16[8,1024]{1,0:T(8,128)(2,1)S(1)}, u32[]{:S(2)}, u32[]{:S(2)}) collective-permute-start(bf16[8,1024]{1,0:T(8,128)(2,1)S(1)} %fusion.212), channel_id=1, source_target_pairs={{0,8},{8,16},{16,24},{24,32},{32,40},{40,48},{48,56},{56,64},{64,7... | collective-permute-start | bytes 49160 | tf_op jit(solution)/shard_map/while/body/eval_jaxpr/ppermute | solution.py:16
  146.2 7.7 %collective-permute-start = (bf16[8,1024]{1,0:T(8,128)(2,1)S(1)}, bf16[8,1024]{1,0:T(8,128)(2,1)S(1)}, u32[]{:S(2)}, u32[]{:S(2)}) collective-permute-start(bf16[8,1024]{1,0:T(8,128)(2,1)S(1)} %fusion.212), channel_id=1, source_target_pairs={{0,8},{8,16},{16,24},{24,32},{32,40},{40,48},{48,56},{56,64},{64,7... | collective-permute-start | bytes 49160 | tf_op jit(solution)/shard_map/while/body/eval_jaxpr/ppermute | solution.py:16
  154.7 7.7 %collective-permute-start = (bf16[8,1024]{1,0:T(8,128)(2,1)S(1)}, bf16[8,1024]{1,0:T(8,128)(2,1)S(1)}, u32[]{:S(2)}, u32[]{:S(2)}) collective-permute-start(bf16[8,1024]{1,0:T(8,128)(2,1)S(1)} %fusion.212), channel_id=1, source_target_pairs={{0,8},{8,16},{16,24},{24,32},{32,40},{40,48},{48,56},{56,64},{64,7... | collective-permute-start | bytes 49160 | tf_op jit(solution)/shard_map/while/body/eval_jaxpr/ppermute | solution.py:16
  163.1 7.7 %collective-permute-start = (bf16[8,1024]{1,0:T(8,128)(2,1)S(1)}, bf16[8,1024]{1,0:T(8,128)(2,1)S(1)}, u32[]{:S(2)}, u32[]{:S(2)}) collective-permute-start(bf16[8,1024]{1,0:T(8,128)(2,1)S(1)} %fusion.212), channel_id=1, source_target_pairs={{0,8},{8,16},{16,24},{24,32},{32,40},{40,48},{48,56},{56,64},{64,7... | collective-permute-start | bytes 49160 | tf_op jit(solution)/shard_map/while/body/eval_jaxpr/ppermute | solution.py:16
  186.1 77.5 %all-gather.9.cloned.1.call-start = ((), (), s32[]{:S(2)}) async-start(), calls=%async_computation.1 | async-start | bytes 4718592 | tf_op jit(solution)/shard_map/all_gather | solution.py:151
  188.9 148.8 %all-gather.15.cloned.1.call-start = ((), (), s32[]{:S(2)}) async-start(), calls=%async_computation.5 | async-start | bytes 8912896 | tf_op jit(solution)/shard_map/all_gather | solution.py:156
  229.3 181.4 %all-gather.13.cloned.1.call-start = ((), (), s32[]{:S(2)}) async-start(), calls=%async_computation.4 | async-start | bytes 8912896 | tf_op jit(solution)/shard_map/all_gather | solution.py:157
  268.1 193.0 %all-reduce.3.cloned.1.call-start = ((), (), s32[]{:S(2)}) async-start(), calls=%async_computation.7 | async-start | bytes 6291456 | tf_op jit(solution)/shard_map/psum | solution.py:168
  432.2 141.1 %reduce-scatter.2.cloned.1.call-start = ((), (), s32[]{:S(2)}) async-start(), calls=%async_computation.3 | async-start | bytes 8912896 | tf_op jit(solution)/shard_map/reduce_scatter | solution.py:186
  486.2 87.2 %copy-start.44 = (bf16[1024,768]{1,0:T(8,128)(2,1)S(1)}, bf16[1024,768]{1,0:T(8,128)(2,1)}, u32[]{:S(2)}) copy-start(bf16[1024,768]{1,0:T(8,128)(2,1)} %get-tuple-element.97) | copy-start | bytes 4718596
  486.3 120.8 %all-gather.17.cloned.1.call-start = ((), (), s32[]{:S(2)}) async-start(), calls=%async_computation.6 | async-start | bytes 4718592 | tf_op jit(solution)/shard_map/all_gather | solution.py:192
  573.4 7.9 %copy-start.6 = (bf16[8,128,2048]{2,1,0:T(8,128)(2,1)S(1)}, bf16[8,128,2048]{2,1,0:T(8,128)(2,1)}, u32[]{:S(2)}) copy-start(bf16[8,128,2048]{2,1,0:T(8,128)(2,1)} %copy-done.5) | copy-start | bytes 12582916
  573.4 7.9 %copy-start.45 = (bf16[1024,768]{1,0:T(8,128)(2,1)S(1)}, bf16[1024,768]{1,0:T(8,128)(2,1)}, u32[]{:S(2)}) copy-start(bf16[1024,768]{1,0:T(8,128)(2,1)} %get-tuple-element.98) | copy-start | bytes 4718596
  587.4 22.8 %copy-start.4 = (bf16[1024,512]{1,0:T(8,128)(2,1)S(1)}, bf16[1024,512]{1,0:T(8,128)(2,1)}, u32[]{:S(2)}) copy-start(bf16[1024,512]{1,0:T(8,128)(2,1)} %param.14) | copy-start | bytes 3145732
  633.0 121.2 %copy-start.27 = (f32[1024,8]{0,1:T(8,128)S(1)}, f32[1024,8]{0,1:T(8,128)}, u32[]{:S(2)}) copy-start(f32[1024,8]{0,1:T(8,128)} %get-tuple-element.107) | copy-start | bytes 98308
  633.0 121.2 %copy-start.37 = (f32[8]{0:T(128)S(1)}, f32[8]{0:T(128)}, u32[]{:S(2)}) copy-start(f32[8]{0:T(128)} %get-tuple-element.120) | copy-start | bytes 100
  636.9 7.7 %collective-permute-start.1 = (bf16[8,1024]{1,0:T(8,128)(2,1)S(1)}, bf16[8,1024]{1,0:T(8,128)(2,1)S(1)}, u32[]{:S(2)}, u32[]{:S(2)}) collective-permute-start(bf16[8,1024]{1,0:T(8,128)(2,1)S(1)} %fusion.213), channel_id=1, source_target_pairs={{8,0},{16,8},{24,16},{32,24},{40,32},{48,40},{56,48},{64,56},{72,6... | collective-permute-start | bytes 49160 | tf_op jit(solution)/shard_map/while/body/eval_jaxpr/ppermute | solution.py:16
  644.7 7.7 %collective-permute-start.1 = (bf16[8,1024]{1,0:T(8,128)(2,1)S(1)}, bf16[8,1024]{1,0:T(8,128)(2,1)S(1)}, u32[]{:S(2)}, u32[]{:S(2)}) collective-permute-start(bf16[8,1024]{1,0:T(8,128)(2,1)S(1)} %fusion.213), channel_id=1, source_target_pairs={{8,0},{16,8},{24,16},{32,24},{40,32},{48,40},{56,48},{64,56},{72,6... | collective-permute-start | bytes 49160 | tf_op jit(solution)/shard_map/while/body/eval_jaxpr/ppermute | solution.py:16
  652.5 7.7 %collective-permute-start.1 = (bf16[8,1024]{1,0:T(8,128)(2,1)S(1)}, bf16[8,1024]{1,0:T(8,128)(2,1)S(1)}, u32[]{:S(2)}, u32[]{:S(2)}) collective-permute-start(bf16[8,1024]{1,0:T(8,128)(2,1)S(1)} %fusion.213), channel_id=1, source_target_pairs={{8,0},{16,8},{24,16},{32,24},{40,32},{48,40},{56,48},{64,56},{72,6... | collective-permute-start | bytes 49160 | tf_op jit(solution)/shard_map/while/body/eval_jaxpr/ppermute | solution.py:16
  660.3 7.7 %collective-permute-start.1 = (bf16[8,1024]{1,0:T(8,128)(2,1)S(1)}, bf16[8,1024]{1,0:T(8,128)(2,1)S(1)}, u32[]{:S(2)}, u32[]{:S(2)}) collective-permute-start(bf16[8,1024]{1,0:T(8,128)(2,1)S(1)} %fusion.213), channel_id=1, source_target_pairs={{8,0},{16,8},{24,16},{32,24},{40,32},{48,40},{56,48},{64,56},{72,6... | collective-permute-start | bytes 49160 | tf_op jit(solution)/shard_map/while/body/eval_jaxpr/ppermute | solution.py:16
  668.1 7.7 %collective-permute-start.1 = (bf16[8,1024]{1,0:T(8,128)(2,1)S(1)}, bf16[8,1024]{1,0:T(8,128)(2,1)S(1)}, u32[]{:S(2)}, u32[]{:S(2)}) collective-permute-start(bf16[8,1024]{1,0:T(8,128)(2,1)S(1)} %fusion.213), channel_id=1, source_target_pairs={{8,0},{16,8},{24,16},{32,24},{40,32},{48,40},{56,48},{64,56},{72,6... | collective-permute-start | bytes 49160 | tf_op jit(solution)/shard_map/while/body/eval_jaxpr/ppermute | solution.py:16
  675.9 7.7 %collective-permute-start.1 = (bf16[8,1024]{1,0:T(8,128)(2,1)S(1)}, bf16[8,1024]{1,0:T(8,128)(2,1)S(1)}, u32[]{:S(2)}, u32[]{:S(2)}) collective-permute-start(bf16[8,1024]{1,0:T(8,128)(2,1)S(1)} %fusion.213), channel_id=1, source_target_pairs={{8,0},{16,8},{24,16},{32,24},{40,32},{48,40},{56,48},{64,56},{72,6... | collective-permute-start | bytes 49160 | tf_op jit(solution)/shard_map/while/body/eval_jaxpr/ppermute | solution.py:16
  683.7 7.7 %collective-permute-start.1 = (bf16[8,1024]{1,0:T(8,128)(2,1)S(1)}, bf16[8,1024]{1,0:T(8,128)(2,1)S(1)}, u32[]{:S(2)}, u32[]{:S(2)}) collective-permute-start(bf16[8,1024]{1,0:T(8,128)(2,1)S(1)} %fusion.213), channel_id=1, source_target_pairs={{8,0},{16,8},{24,16},{32,24},{40,32},{48,40},{56,48},{64,56},{72,6... | collective-permute-start | bytes 49160 | tf_op jit(solution)/shard_map/while/body/eval_jaxpr/ppermute | solution.py:16
  691.6 7.7 %collective-permute-start.1 = (bf16[8,1024]{1,0:T(8,128)(2,1)S(1)}, bf16[8,1024]{1,0:T(8,128)(2,1)S(1)}, u32[]{:S(2)}, u32[]{:S(2)}) collective-permute-start(bf16[8,1024]{1,0:T(8,128)(2,1)S(1)} %fusion.213), channel_id=1, source_target_pairs={{8,0},{16,8},{24,16},{32,24},{40,32},{48,40},{56,48},{64,56},{72,6... | collective-permute-start | bytes 49160 | tf_op jit(solution)/shard_map/while/body/eval_jaxpr/ppermute | solution.py:16
  699.4 7.7 %collective-permute-start.1 = (bf16[8,1024]{1,0:T(8,128)(2,1)S(1)}, bf16[8,1024]{1,0:T(8,128)(2,1)S(1)}, u32[]{:S(2)}, u32[]{:S(2)}) collective-permute-start(bf16[8,1024]{1,0:T(8,128)(2,1)S(1)} %fusion.213), channel_id=1, source_target_pairs={{8,0},{16,8},{24,16},{32,24},{40,32},{48,40},{56,48},{64,56},{72,6... | collective-permute-start | bytes 49160 | tf_op jit(solution)/shard_map/while/body/eval_jaxpr/ppermute | solution.py:16
  707.2 7.7 %collective-permute-start.1 = (bf16[8,1024]{1,0:T(8,128)(2,1)S(1)}, bf16[8,1024]{1,0:T(8,128)(2,1)S(1)}, u32[]{:S(2)}, u32[]{:S(2)}) collective-permute-start(bf16[8,1024]{1,0:T(8,128)(2,1)S(1)} %fusion.213), channel_id=1, source_target_pairs={{8,0},{16,8},{24,16},{32,24},{40,32},{48,40},{56,48},{64,56},{72,6... | collective-permute-start | bytes 49160 | tf_op jit(solution)/shard_map/while/body/eval_jaxpr/ppermute | solution.py:16
  715.0 7.7 %collective-permute-start.1 = (bf16[8,1024]{1,0:T(8,128)(2,1)S(1)}, bf16[8,1024]{1,0:T(8,128)(2,1)S(1)}, u32[]{:S(2)}, u32[]{:S(2)}) collective-permute-start(bf16[8,1024]{1,0:T(8,128)(2,1)S(1)} %fusion.213), channel_id=1, source_target_pairs={{8,0},{16,8},{24,16},{32,24},{40,32},{48,40},{56,48},{64,56},{72,6... | collective-permute-start | bytes 49160 | tf_op jit(solution)/shard_map/while/body/eval_jaxpr/ppermute | solution.py:16
  722.8 7.8 %collective-permute-start.1 = (bf16[8,1024]{1,0:T(8,128)(2,1)S(1)}, bf16[8,1024]{1,0:T(8,128)(2,1)S(1)}, u32[]{:S(2)}, u32[]{:S(2)}) collective-permute-start(bf16[8,1024]{1,0:T(8,128)(2,1)S(1)} %fusion.213), channel_id=1, source_target_pairs={{8,0},{16,8},{24,16},{32,24},{40,32},{48,40},{56,48},{64,56},{72,6... | collective-permute-start | bytes 49160 | tf_op jit(solution)/shard_map/while/body/eval_jaxpr/ppermute | solution.py:16
  730.7 7.7 %collective-permute-start.1 = (bf16[8,1024]{1,0:T(8,128)(2,1)S(1)}, bf16[8,1024]{1,0:T(8,128)(2,1)S(1)}, u32[]{:S(2)}, u32[]{:S(2)}) collective-permute-start(bf16[8,1024]{1,0:T(8,128)(2,1)S(1)} %fusion.213), channel_id=1, source_target_pairs={{8,0},{16,8},{24,16},{32,24},{40,32},{48,40},{56,48},{64,56},{72,6... | collective-permute-start | bytes 49160 | tf_op jit(solution)/shard_map/while/body/eval_jaxpr/ppermute | solution.py:16
  738.5 7.7 %collective-permute-start.1 = (bf16[8,1024]{1,0:T(8,128)(2,1)S(1)}, bf16[8,1024]{1,0:T(8,128)(2,1)S(1)}, u32[]{:S(2)}, u32[]{:S(2)}) collective-permute-start(bf16[8,1024]{1,0:T(8,128)(2,1)S(1)} %fusion.213), channel_id=1, source_target_pairs={{8,0},{16,8},{24,16},{32,24},{40,32},{48,40},{56,48},{64,56},{72,6... | collective-permute-start | bytes 49160 | tf_op jit(solution)/shard_map/while/body/eval_jaxpr/ppermute | solution.py:16
  746.4 7.7 %collective-permute-start.1 = (bf16[8,1024]{1,0:T(8,128)(2,1)S(1)}, bf16[8,1024]{1,0:T(8,128)(2,1)S(1)}, u32[]{:S(2)}, u32[]{:S(2)}) collective-permute-start(bf16[8,1024]{1,0:T(8,128)(2,1)S(1)} %fusion.213), channel_id=1, source_target_pairs={{8,0},{16,8},{24,16},{32,24},{40,32},{48,40},{56,48},{64,56},{72,6... | collective-permute-start | bytes 49160 | tf_op jit(solution)/shard_map/while/body/eval_jaxpr/ppermute | solution.py:16
  756.6 7.1 copy-start.1
  (36 other events, 136.8 us)
Sparse Core Ops, SparseCore 0:
  186.2 38.4 all-gather.10
  227.0 36.5 all-gather.8
  266.2 71.4 all-gather.14
  340.3 70.3 all-gather.12
  432.3 28.7 all-reduce.2
  486.4 86.8 reduce-scatter.1
  575.0 31.9 all-gather.16
where the time goes:
time: 781 us; the launch traced here: 771 us
  waiting for transfers between devices  434 us (56%)
  starting transfers between devices  121 us (15%)
  matrix products  119 us (15%)
  local copies, waits for them, and re-layouts  54.2 us (7%)
  other arithmetic  26.6 us (3%)
  between operations  15.5 us (2%)
    ppermute x30, starting transfers between devices, from_behind(): lax.ppermute(value, axis, [(source, source + steps) for source in range(f...  120 us
    ppermute x30, waiting for transfers between devices, from_behind(): lax.ppermute(value, axis, [(source, source + steps) for source in range(f...  109 us
    reduce_scatter x1, waiting for transfers between devices, per_device(): lax.psum_scatter(spread_rows.reshape(BLOCK * lax.axis_size('seq'), half_w...  87 us
    all_gather x1, waiting for transfers between devices, per_device(): lax.all_gather(h_block, 'seq', axis=0, tiled=True)  69 us
    all_gather x1, waiting for transfers between devices, per_device(): lax.all_gather(g_block, 'seq', axis=0, tiled=True)  51.2 us
    all_gather x1, waiting for transfers between devices, per_device(): lax.all_gather(h_pick, ('expert', 'mp'), axis=2, tiled=True)  35.8 us
    all_gather x1, waiting for transfers between devices, per_device(): lax.all_gather(g_pick, ('expert', 'mp'), axis=2, tiled=True)  34.2 us
    psum x1, waiting for transfers between devices, per_device(): lax.psum(rounded(jnp.dot(x_rows, up_local, preferred_element_type=jnp.flo...  28.9 us
  transfers between devices with their start and end apart: 37, of which 37 were waited for; matrix products, arithmetic and copies ran while one was open for 6% of the time, Pallas kernels for 0%

commit v1 on v0

--- a/solution.py
+++ b/solution.py
@@ -8,6 +8,12 @@
 BLOCK = 128
 spike_position_step = 0.3
 highest = lax.Precision.HIGHEST
+
+
+def _scan_state(v0, a_name):
+    after = jnp.concatenate([v0] * jax.lax.axis_size(a_name), 2)
+    even = jax.lax.all_to_all(after, a_name, 2, 2, tiled=True)
+    return even
 
 
 def from_behind(value, axis, steps):
@@ -147,7 +153,7 @@
         preferred_element_type=jnp.float32,
     ).astype(jnp.bfloat16)
     h_full, g_full = (
-        lax.all_gather(h_pick, ("expert", "mp"), axis=2, tiled=True),
+        _scan_state(h_pick, ("expert", "mp")),
         lax.all_gather(g_pick, ("expert", "mp"), axis=2, tiled=True),
     )
     h_block = narrow(h_full, exp_index, mp_index, half_width)

time: 781 us -> 772 us (0.988)
  waiting for transfers between devices: 434 us -> 410 us
  local copies, waits for them, and re-layouts: 54.2 us -> 73.1 us
    all_to_all x0 -> x1, waiting for transfers between devices: none -> 49.7 us  [_scan_state(): even = jax.lax.all_to_all(after, a_name, 2, 2, tiled=True)]
    all_gather x1 -> x0, waiting for transfers between devices: 35.8 us -> none  [per_device(): lax.all_gather(h_pick, ('expert', 'mp'), axis=2, tiled=True)]
    all_gather x1, waiting for transfers between devices: 34.2 us -> 0.02 us  [per_device(): lax.all_gather(g_pick, ('expert', 'mp'), axis=2, tiled=True)]
    concatenate x0 -> x2, local copies, waits for them, and re-layouts: none -> 10.6 us  [_scan_state(): after = jnp.concatenate([v0] * jax.lax.axis_size(a_name), 2)]
  transfers between devices with their start and end apart: 37 -> 37, of which waited for: 37 -> 36; matrix products, arithmetic and copies ran while one was open for 6% -> 16% of each run, Pallas kernels for 0% -> 0%
where the time goes in v1:
time: 772 us; the launch traced here: 765 us
  waiting for transfers between devices  410 us (53%)
  starting transfers between devices  126 us (16%)
  matrix products  113 us (15%)
  local copies, waits for them, and re-layouts  73.1 us (9%)
  other arithmetic  26.4 us (3%)
  between operations  15.7 us (2%)
    ppermute x30, starting transfers between devices, from_behind(): lax.ppermute(value, axis, [(source, source + steps) for source in range(f...  120 us
    ppermute x30, waiting for transfers between devices, from_behind(): lax.ppermute(value, axis, [(source, source + steps) for source in range(f...  109 us
    reduce_scatter x1, waiting for transfers between devices, per_device(): lax.psum_scatter(spread_rows.reshape(BLOCK * lax.axis_size('seq'), half_w...  87 us
    all_gather x1, waiting for transfers between devices, per_device(): lax.all_gather(h_block, 'seq', axis=0, tiled=True)  65.2 us
    all_gather x1, waiting for transfers between devices, per_device(): lax.all_gather(g_block, 'seq', axis=0, tiled=True)  51.1 us
    all_to_all x1, waiting for transfers between devices, _scan_state(): even = jax.lax.all_to_all(after, a_name, 2, 2, tiled=True)  49.7 us
    psum x1, waiting for transfers between devices, per_device(): lax.psum(rounded(jnp.dot(x_rows, up_local, preferred_element_type=jnp.flo...  28.9 us
    dot_general x2, matrix products, compact(): jnp.einsum('js,srf->jrf', select, shaped, preferred_element_type=jnp.floa...  25 us
  transfers between devices with their start and end apart: 37, of which 36 were waited for; matrix products, arithmetic and copies ran while one was open for 16% of the time, Pallas kernels for 0%

profile of v1, /device:TPU:6, one launch (start us, length us, event | category | flops | bytes accessed | tf_op | source)
XLA Modules:
  0.0 764.5 jit_solution(15535578040482635477)
XLA Ops:
  39.2 123.7 %while.22 = (s32[]{:T(128)}, f32[8,1024]{1,0:T(8,128)S(1)}, f32[8]{0:T(128)}, f32[8,1024]{1,0:T(8,128)S(1)}, s32[]{:T(128)}, /*index=5*/s32[]{:T(128)}) while((s32[]{:T(128)}, f32[8,1024]{1,0:T(8,128)S(1)}, f32[8]{0:T(128)}, f32[8,1024]{1,0:T(8,128)S(1)}, s32[]{:T(128)}, /*index=5*/s32[]{:T(128)}) %tuple.60), condition=%wide.region_6.7_spmd.clone, body=%wide.region_5.6_spmd.clone.sunk | while | flops 40963 | bytes 196759 | solution.py:131
  46.3 5.5 collective-permute-start
  53.9 6.3 collective-permute-start
  62.3 6.3 collective-permute-start
  70.7 6.3 collective-permute-start
  79.2 6.3 collective-permute-start
  87.6 6.3 collective-permute-start
  96.0 6.3 collective-permute-start
  104.5 6.3 collective-permute-start
  112.9 6.3 collective-permute-start
  121.3 6.3 collective-permute-start
  129.8 6.3 collective-permute-start
  138.2 6.3 collective-permute-start
  146.6 6.3 collective-permute-start
  155.0 6.3 collective-permute-start
  189.9 9.6 %copy.180 = bf16[4,128,4096]{1,0,2:T(4,128)(2,1)} copy(bf16[4,128,4096]{2,0,1:T(4,128)(2,1)} %constant_dynamic-update-slice_fusion) | data formatting | bytes 8388608 | tf_op jit(solution)/shard_map/concatenate | solution.py:14
  199.5 5.3 all-to-all-start
  204.8 49.7 %all-to-all-done = bf16[4,128,4096]{1,0,2:T(4,128)(2,1)} async-done(((bf16[4,128,4096]{1,0,2:T(4,128)(2,1)}), bf16[4,128,4096]{1,0,2:T(4,128)(2,1)}, u32[]{:S(2)}, u32[]{:S(2)}) %all-to-all-start) | async-done | bytes 4194336 | tf_op jit(solution)/shard_map/all_to_all | solution.py:15
  266.6 65.2 %all-gather.12.cloned.1.call-done = bf16[1,2048,2048]{2,1,0:T(8,128)(2,1)} async-done(((bf16[1,128,2048]{2,1,0:T(8,128)(2,1)}), bf16[1,2048,2048]{2,1,0:T(8,128)(2,1)}) %all-gather.12.cloned.1.call-update) | async-done | bytes 8388624 | tf_op jit(solution)/shard_map/all_gather | solution.py:162
  331.8 12.5 %fusion.56 = bf16[8,128,2048]{2,0,1:T(8,128)(2,1)S(1)} fusion(bf16[16,128,2048]{2,1,0:T(8,128)(2,1)} %bitcast.155, s32[16]{0:T(128)S(1)} %add_reduce_fusion, pred[16]{0:T(512)(128)(4,1)S(1)} %compare_reduce_fusion), kind=kOutput, calls=%fused_computation.58 | convolution fusion | flops 69206272 | bytes 12582992 | tf_op jit(solution)/shard_map/js,srf->jrf/dot_general | solution.py:48
  348.8 4.5 fusion.79
  353.3 51.1 %all-gather.10.cloned.1.call-done = bf16[1,2048,2048]{2,1,0:T(8,128)(2,1)} async-done(((bf16[1,128,2048]{2,1,0:T(8,128)(2,1)}), bf16[1,2048,2048]{2,1,0:T(8,128)(2,1)}) %all-gather.10.cloned.1.call-update) | async-done | bytes 8388624 | tf_op jit(solution)/shard_map/all_gather | solution.py:163
  404.4 12.5 %fusion.53 = bf16[8,128,2048]{2,0,1:T(8,128)(2,1)S(1)} fusion(bf16[16,128,2048]{2,1,0:T(8,128)(2,1)} %bitcast.156, s32[16]{0:T(128)S(1)} %add_reduce_fusion, pred[16]{0:T(512)(128)(4,1)S(1)} %compare_reduce_fusion), kind=kOutput, calls=%fused_computation.57 | convolution fusion | flops 69206272 | bytes 12582992 | tf_op jit(solution)/shard_map/js,srf->jrf/dot_general | solution.py:48
  421.5 4.6 fusion.76
  426.2 28.9 %all-reduce.3.cloned.1.call-done = (bf16[1024,768]{1,0:T(8,128)(2,1)}, bf16[1024,768]{1,0:T(8,128)(2,1)}) async-done(((bf16[1024,768]{1,0:T(8,128)(2,1)}, bf16[1024,768]{1,0:T(8,128)(2,1)}), (bf16[1024,768]{1,0:T(8,128)(2,1)}, bf16[1024,768]{1,0:T(8,128)(2,1)})) %all-reduce.3.cloned.1.call-update) | async-done | bytes 3145744 | tf_op jit(solution)/shard_map/psum | solution.py:174
  455.0 6.9 convolution_convert_fusion.1
  462.0 6.9 convolution_convert_fusion
  468.9 11.3 %copy.185 = bf16[16,128,2048]{2,1,0:T(8,128)(2,1)} copy(bf16[16,128,2048]{2,0,1:T(8,128)(2,1)} %convolution_convert_fusion) | data formatting | bytes 16777216 | tf_op jit(solution)/shard_map/convert_element_type | solution.py:193
  480.2 87.0 %reduce-scatter.2.cloned.1.call-done = bf16[128,2048]{1,0:T(8,128)(2,1)} async-done(((bf16[2048,2048]{1,0:T(8,128)(2,1)}), bf16[128,2048]{1,0:T(8,128)(2,1)}) %reduce-scatter.2.cloned.1.call-update) | async-done | bytes 524304 | tf_op jit(solution)/shard_map/reduce_scatter | solution.py:192
  567.4 7.8 %convolution_bitcast_fusion = f32[1,768,2048]{2,1,0:T(8,128)} fusion(bf16[1024,2048]{1,0:T(8,128)(2,1)} %bitcast.165, bf16[1024,768]{1,0:T(8,128)(2,1)S(1)} %copy-done.51), kind=kOutput, calls=%fused_computation.59 | convolution fusion | flops 3225944064 | bytes 12058624 | tf_op jit(solution)/shard_map/tf,td->fd/dot_general | solution.py:179
  575.2 6.1 convolution_bitcast_fusion.1
  581.3 19.5 %all-gather.14.cloned.1.call-done = bf16[1024,2048]{1,0:T(8,128)(2,1)} async-done(((bf16[128,2048]{1,0:T(8,128)(2,1)}), bf16[1024,2048]{1,0:T(8,128)(2,1)}) %all-gather.14.cloned.1.call-update) | async-done | bytes 4194320 | tf_op jit(solution)/shard_map/all_gather | solution.py:198
  630.5 117.3 %while.23 = (s32[]{:T(128)}, f32[8,1024]{1,0:T(8,128)S(1)}, f32[8]{0:T(128)S(1)}, f32[8,1024]{1,0:T(8,128)S(1)}, s32[]{:T(128)}, /*index=5*/s32[]{:T(128)}) while((s32[]{:T(128)}, f32[8,1024]{1,0:T(8,128)S(1)}, f32[8]{0:T(128)S(1)}, f32[8,1024]{1,0:T(8,128)S(1)}, s32[]{:T(128)}, /*index=5*/s32[]{:T(128)}) %tuple.79), condition=%wide.region_10.11_spmd.clone, body=%wide.region_9.10_spmd.clone.sunk | while | flops 40963 | bytes 196759 | solution.py:250
  633.4 5.0 collective-permute-done.1
  640.3 5.8 collective-permute-done.1
  648.2 5.8 collective-permute-done.1
  656.0 5.8 collective-permute-done.1
  663.8 5.8 collective-permute-done.1
  671.6 5.8 collective-permute-done.1
  679.4 5.8 collective-permute-done.1
  687.2 5.8 collective-permute-done.1
  695.0 5.8 collective-permute-done.1
  702.8 5.8 collective-permute-done.1
  710.7 5.8 collective-permute-done.1
  718.5 5.9 collective-permute-done.1
  726.4 5.8 collective-permute-done.1
  734.2 5.8 collective-permute-done.1
  742.0 5.8 collective-permute-done.1
  (293 shorter events, 185.2 us)
Async XLA Ops:
  7.2 341.6 %copy-start = (bf16[1,2048,768]{2,1,0:T(8,128)(2,1)S(1)}, bf16[1,2048,768]{2,1,0:T(8,128)(2,1)}, u32[]{:S(2)}) copy-start(bf16[1,2048,768]{2,1,0:T(8,128)(2,1)} %param.20) | copy-start | bytes 9437188
  7.2 8.8 %copy-start.39 = (s32[1024]{0:T(1024)S(1)}, s32[1024]{0:T(1024)}, u32[]{:S(2)}) copy-start(s32[1024]{0:T(1024)} %param.18) | copy-start | bytes 12292
  7.2 8.8 %copy-start.53 = (f32[8]{0:T(128)S(1)}, f32[8]{0:T(128)}, u32[]{:S(2)}) copy-start(f32[8]{0:T(128)} %param.17) | copy-start | bytes 100
  7.2 13.6 %copy-start.14 = (bf16[1024,16]{0,1:T(8,128)(2,1)S(1)}, bf16[1024,16]{0,1:T(8,128)(2,1)}, u32[]{:S(2)}) copy-start(bf16[1024,16]{0,1:T(8,128)(2,1)} %param.15) | copy-start | bytes 98308
  7.2 13.6 %copy-start.12 = (bf16[1024,16]{0,1:T(8,128)(2,1)S(1)}, bf16[1024,16]{0,1:T(8,128)(2,1)}, u32[]{:S(2)}) copy-start(bf16[1024,16]{0,1:T(8,128)(2,1)} %param.16) | copy-start | bytes 98308
  7.2 253.9 %all-gather.8.cloned.1.call-start = ((), (), s32[]{:S(2)}) async-start(), calls=%async_computation.2 | async-start | bytes 4718592 | tf_op jit(solution)/shard_map/all_gather | solution.py:157
  11.1 21.3 %copy-start.19 = (pred[512,512]{1,0:T(8,128)(4,1)}, pred[512,512]{1,0:T(8,128)(4,1)S(1)}, u32[]{:S(2)}) copy-start(pred[512,512]{1,0:T(8,128)(4,1)S(1)} %iota_compare_fusion) | copy-start | bytes 786436
  39.9 5.6 collective-permute-start
  46.3 6.9 collective-permute-start
  53.9 7.7 %collective-permute-start = (bf16[8,1024]{1,0:T(8,128)(2,1)S(1)}, bf16[8,1024]{1,0:T(8,128)(2,1)S(1)}, u32[]{:S(2)}, u32[]{:S(2)}) collective-permute-start(bf16[8,1024]{1,0:T(8,128)(2,1)S(1)} %fusion.212), channel_id=1, source_target_pairs={{0,8},{8,16},{16,24},{24,32},{32,40},{40,48},{48,56},{56,64},{64,7... | collective-permute-start | bytes 49160 | tf_op jit(solution)/shard_map/while/body/eval_jaxpr/ppermute | solution.py:22
  62.3 7.7 %collective-permute-start = (bf16[8,1024]{1,0:T(8,128)(2,1)S(1)}, bf16[8,1024]{1,0:T(8,128)(2,1)S(1)}, u32[]{:S(2)}, u32[]{:S(2)}) collective-permute-start(bf16[8,1024]{1,0:T(8,128)(2,1)S(1)} %fusion.212), channel_id=1, source_target_pairs={{0,8},{8,16},{16,24},{24,32},{32,40},{40,48},{48,56},{56,64},{64,7... | collective-permute-start | bytes 49160 | tf_op jit(solution)/shard_map/while/body/eval_jaxpr/ppermute | solution.py:22
  70.7 7.7 %collective-permute-start = (bf16[8,1024]{1,0:T(8,128)(2,1)S(1)}, bf16[8,1024]{1,0:T(8,128)(2,1)S(1)}, u32[]{:S(2)}, u32[]{:S(2)}) collective-permute-start(bf16[8,1024]{1,0:T(8,128)(2,1)S(1)} %fusion.212), channel_id=1, source_target_pairs={{0,8},{8,16},{16,24},{24,32},{32,40},{40,48},{48,56},{56,64},{64,7... | collective-permute-start | bytes 49160 | tf_op jit(solution)/shard_map/while/body/eval_jaxpr/ppermute | solution.py:22
  79.2 7.7 %collective-permute-start = (bf16[8,1024]{1,0:T(8,128)(2,1)S(1)}, bf16[8,1024]{1,0:T(8,128)(2,1)S(1)}, u32[]{:S(2)}, u32[]{:S(2)}) collective-permute-start(bf16[8,1024]{1,0:T(8,128)(2,1)S(1)} %fusion.212), channel_id=1, source_target_pairs={{0,8},{8,16},{16,24},{24,32},{32,40},{40,48},{48,56},{56,64},{64,7... | collective-permute-start | bytes 49160 | tf_op jit(solution)/shard_map/while/body/eval_jaxpr/ppermute | solution.py:22
  87.6 7.7 %collective-permute-start = (bf16[8,1024]{1,0:T(8,128)(2,1)S(1)}, bf16[8,1024]{1,0:T(8,128)(2,1)S(1)}, u32[]{:S(2)}, u32[]{:S(2)}) collective-permute-start(bf16[8,1024]{1,0:T(8,128)(2,1)S(1)} %fusion.212), channel_id=1, source_target_pairs={{0,8},{8,16},{16,24},{24,32},{32,40},{40,48},{48,56},{56,64},{64,7... | collective-permute-start | bytes 49160 | tf_op jit(solution)/shard_map/while/body/eval_jaxpr/ppermute | solution.py:22
  96.0 7.7 %collective-permute-start = (bf16[8,1024]{1,0:T(8,128)(2,1)S(1)}, bf16[8,1024]{1,0:T(8,128)(2,1)S(1)}, u32[]{:S(2)}, u32[]{:S(2)}) collective-permute-start(bf16[8,1024]{1,0:T(8,128)(2,1)S(1)} %fusion.212), channel_id=1, source_target_pairs={{0,8},{8,16},{16,24},{24,32},{32,40},{40,48},{48,56},{56,64},{64,7... | collective-permute-start | bytes 49160 | tf_op jit(solution)/shard_map/while/body/eval_jaxpr/ppermute | solution.py:22
  104.5 7.7 %collective-permute-start = (bf16[8,1024]{1,0:T(8,128)(2,1)S(1)}, bf16[8,1024]{1,0:T(8,128)(2,1)S(1)}, u32[]{:S(2)}, u32[]{:S(2)}) collective-permute-start(bf16[8,1024]{1,0:T(8,128)(2,1)S(1)} %fusion.212), channel_id=1, source_target_pairs={{0,8},{8,16},{16,24},{24,32},{32,40},{40,48},{48,56},{56,64},{64,7... | collective-permute-start | bytes 49160 | tf_op jit(solution)/shard_map/while/body/eval_jaxpr/ppermute | solution.py:22
  112.9 7.7 %collective-permute-start = (bf16[8,1024]{1,0:T(8,128)(2,1)S(1)}, bf16[8,1024]{1,0:T(8,128)(2,1)S(1)}, u32[]{:S(2)}, u32[]{:S(2)}) collective-permute-start(bf16[8,1024]{1,0:T(8,128)(2,1)S(1)} %fusion.212), channel_id=1, source_target_pairs={{0,8},{8,16},{16,24},{24,32},{32,40},{40,48},{48,56},{56,64},{64,7... | collective-permute-start | bytes 49160 | tf_op jit(solution)/shard_map/while/body/eval_jaxpr/ppermute | solution.py:22
  121.3 7.7 %collective-permute-start = (bf16[8,1024]{1,0:T(8,128)(2,1)S(1)}, bf16[8,1024]{1,0:T(8,128)(2,1)S(1)}, u32[]{:S(2)}, u32[]{:S(2)}) collective-permute-start(bf16[8,1024]{1,0:T(8,128)(2,1)S(1)} %fusion.212), channel_id=1, source_target_pairs={{0,8},{8,16},{16,24},{24,32},{32,40},{40,48},{48,56},{56,64},{64,7... | collective-permute-start | bytes 49160 | tf_op jit(solution)/shard_map/while/body/eval_jaxpr/ppermute | solution.py:22
  129.8 7.7 %collective-permute-start = (bf16[8,1024]{1,0:T(8,128)(2,1)S(1)}, bf16[8,1024]{1,0:T(8,128)(2,1)S(1)}, u32[]{:S(2)}, u32[]{:S(2)}) collective-permute-start(bf16[8,1024]{1,0:T(8,128)(2,1)S(1)} %fusion.212), channel_id=1, source_target_pairs={{0,8},{8,16},{16,24},{24,32},{32,40},{40,48},{48,56},{56,64},{64,7... | collective-permute-start | bytes 49160 | tf_op jit(solution)/shard_map/while/body/eval_jaxpr/ppermute | solution.py:22
  138.2 7.7 %collective-permute-start = (bf16[8,1024]{1,0:T(8,128)(2,1)S(1)}, bf16[8,1024]{1,0:T(8,128)(2,1)S(1)}, u32[]{:S(2)}, u32[]{:S(2)}) collective-permute-start(bf16[8,1024]{1,0:T(8,128)(2,1)S(1)} %fusion.212), channel_id=1, source_target_pairs={{0,8},{8,16},{16,24},{24,32},{32,40},{40,48},{48,56},{56,64},{64,7... | collective-permute-start | bytes 49160 | tf_op jit(solution)/shard_map/while/body/eval_jaxpr/ppermute | solution.py:22
  146.6 7.7 %collective-permute-start = (bf16[8,1024]{1,0:T(8,128)(2,1)S(1)}, bf16[8,1024]{1,0:T(8,128)(2,1)S(1)}, u32[]{:S(2)}, u32[]{:S(2)}) collective-permute-start(bf16[8,1024]{1,0:T(8,128)(2,1)S(1)} %fusion.212), channel_id=1, source_target_pairs={{0,8},{8,16},{16,24},{24,32},{32,40},{40,48},{48,56},{56,64},{64,7... | collective-permute-start | bytes 49160 | tf_op jit(solution)/shard_map/while/body/eval_jaxpr/ppermute | solution.py:22
  155.0 7.7 %collective-permute-start = (bf16[8,1024]{1,0:T(8,128)(2,1)S(1)}, bf16[8,1024]{1,0:T(8,128)(2,1)S(1)}, u32[]{:S(2)}, u32[]{:S(2)}) collective-permute-start(bf16[8,1024]{1,0:T(8,128)(2,1)S(1)} %fusion.212), channel_id=1, source_target_pairs={{0,8},{8,16},{16,24},{24,32},{32,40},{40,48},{48,56},{56,64},{64,7... | collective-permute-start | bytes 49160 | tf_op jit(solution)/shard_map/while/body/eval_jaxpr/ppermute | solution.py:22
  199.5 55.0 %all-to-all-start = ((bf16[4,128,4096]{1,0,2:T(4,128)(2,1)}), bf16[4,128,4096]{1,0,2:T(4,128)(2,1)}, u32[]{:S(2)}, u32[]{:S(2)}) async-start(bf16[4,128,4096]{1,0,2:T(4,128)(2,1)} %copy.180), calls=%async_computation | async-start | bytes 8388608 | tf_op jit(solution)/shard_map/all_to_all | solution.py:15
  204.7 127.1 %all-gather.12.cloned.1.call-start = ((), (), s32[]{:S(2)}) async-start(), calls=%async_computation.5 | async-start | bytes 8912896 | tf_op jit(solution)/shard_map/all_gather | solution.py:162
  204.8 61.5 %copy-start.31 = (s32[16,8]{1,0:T(8,128)S(1)}, s32[16,8]{1,0:T(8,128)}, u32[]{:S(2)}) copy-start(s32[16,8]{1,0:T(8,128)} %copy-done.30) | copy-start | bytes 1540
  261.1 143.3 %all-gather.10.cloned.1.call-start = ((), (), s32[]{:S(2)}) async-start(), calls=%async_computation.4 | async-start | bytes 8912896 | tf_op jit(solution)/shard_map/all_gather | solution.py:163
  265.8 189.3 %all-reduce.3.cloned.1.call-start = ((), (), s32[]{:S(2)}) async-start(), calls=%async_computation.7 | async-start | bytes 6291456 | tf_op jit(solution)/shard_map/psum | solution.py:174
  426.1 141.1 %reduce-scatter.2.cloned.1.call-start = ((), (), s32[]{:S(2)}) async-start(), calls=%async_computation.3 | async-start | bytes 8912896 | tf_op jit(solution)/shard_map/reduce_scatter | solution.py:192
  480.2 87.2 %copy-start.51 = (bf16[1024,768]{1,0:T(8,128)(2,1)S(1)}, bf16[1024,768]{1,0:T(8,128)(2,1)}, u32[]{:S(2)}) copy-start(bf16[1024,768]{1,0:T(8,128)(2,1)} %get-tuple-element.97) | copy-start | bytes 4718596
  480.2 120.6 %all-gather.14.cloned.1.call-start = ((), (), s32[]{:S(2)}) async-start(), calls=%async_computation.6 | async-start | bytes 4718592 | tf_op jit(solution)/shard_map/all_gather | solution.py:198
  581.3 22.7 %copy-start.3 = (bf16[1024,512]{1,0:T(8,128)(2,1)S(1)}, bf16[1024,512]{1,0:T(8,128)(2,1)}, u32[]{:S(2)}) copy-start(bf16[1024,512]{1,0:T(8,128)(2,1)} %param.14) | copy-start | bytes 3145732
  626.7 121.2 %copy-start.28 = (f32[1024,8]{0,1:T(8,128)S(1)}, f32[1024,8]{0,1:T(8,128)}, u32[]{:S(2)}) copy-start(f32[1024,8]{0,1:T(8,128)} %get-tuple-element.107) | copy-start | bytes 98308
  626.8 121.2 %copy-start.43 = (f32[8]{0:T(128)S(1)}, f32[8]{0:T(128)}, u32[]{:S(2)}) copy-start(f32[8]{0:T(128)} %get-tuple-element.120) | copy-start | bytes 100
  630.6 7.7 %collective-permute-start.1 = (bf16[8,1024]{1,0:T(8,128)(2,1)S(1)}, bf16[8,1024]{1,0:T(8,128)(2,1)S(1)}, u32[]{:S(2)}, u32[]{:S(2)}) collective-permute-start(bf16[8,1024]{1,0:T(8,128)(2,1)S(1)} %fusion.213), channel_id=1, source_target_pairs={{8,0},{16,8},{24,16},{32,24},{40,32},{48,40},{56,48},{64,56},{72,6... | collective-permute-start | bytes 49160 | tf_op jit(solution)/shard_map/while/body/eval_jaxpr/ppermute | solution.py:22
  638.4 7.7 %collective-permute-start.1 = (bf16[8,1024]{1,0:T(8,128)(2,1)S(1)}, bf16[8,1024]{1,0:T(8,128)(2,1)S(1)}, u32[]{:S(2)}, u32[]{:S(2)}) collective-permute-start(bf16[8,1024]{1,0:T(8,128)(2,1)S(1)} %fusion.213), channel_id=1, source_target_pairs={{8,0},{16,8},{24,16},{32,24},{40,32},{48,40},{56,48},{64,56},{72,6... | collective-permute-start | bytes 49160 | tf_op jit(solution)/shard_map/while/body/eval_jaxpr/ppermute | solution.py:22
  646.2 7.7 %collective-permute-start.1 = (bf16[8,1024]{1,0:T(8,128)(2,1)S(1)}, bf16[8,1024]{1,0:T(8,128)(2,1)S(1)}, u32[]{:S(2)}, u32[]{:S(2)}) collective-permute-start(bf16[8,1024]{1,0:T(8,128)(2,1)S(1)} %fusion.213), channel_id=1, source_target_pairs={{8,0},{16,8},{24,16},{32,24},{40,32},{48,40},{56,48},{64,56},{72,6... | collective-permute-start | bytes 49160 | tf_op jit(solution)/shard_map/while/body/eval_jaxpr/ppermute | solution.py:22
  654.1 7.7 %collective-permute-start.1 = (bf16[8,1024]{1,0:T(8,128)(2,1)S(1)}, bf16[8,1024]{1,0:T(8,128)(2,1)S(1)}, u32[]{:S(2)}, u32[]{:S(2)}) collective-permute-start(bf16[8,1024]{1,0:T(8,128)(2,1)S(1)} %fusion.213), channel_id=1, source_target_pairs={{8,0},{16,8},{24,16},{32,24},{40,32},{48,40},{56,48},{64,56},{72,6... | collective-permute-start | bytes 49160 | tf_op jit(solution)/shard_map/while/body/eval_jaxpr/ppermute | solution.py:22
  661.9 7.7 %collective-permute-start.1 = (bf16[8,1024]{1,0:T(8,128)(2,1)S(1)}, bf16[8,1024]{1,0:T(8,128)(2,1)S(1)}, u32[]{:S(2)}, u32[]{:S(2)}) collective-permute-start(bf16[8,1024]{1,0:T(8,128)(2,1)S(1)} %fusion.213), channel_id=1, source_target_pairs={{8,0},{16,8},{24,16},{32,24},{40,32},{48,40},{56,48},{64,56},{72,6... | collective-permute-start | bytes 49160 | tf_op jit(solution)/shard_map/while/body/eval_jaxpr/ppermute | solution.py:22
  669.7 7.7 %collective-permute-start.1 = (bf16[8,1024]{1,0:T(8,128)(2,1)S(1)}, bf16[8,1024]{1,0:T(8,128)(2,1)S(1)}, u32[]{:S(2)}, u32[]{:S(2)}) collective-permute-start(bf16[8,1024]{1,0:T(8,128)(2,1)S(1)} %fusion.213), channel_id=1, source_target_pairs={{8,0},{16,8},{24,16},{32,24},{40,32},{48,40},{56,48},{64,56},{72,6... | collective-permute-start | bytes 49160 | tf_op jit(solution)/shard_map/while/body/eval_jaxpr/ppermute | solution.py:22
  677.5 7.7 %collective-permute-start.1 = (bf16[8,1024]{1,0:T(8,128)(2,1)S(1)}, bf16[8,1024]{1,0:T(8,128)(2,1)S(1)}, u32[]{:S(2)}, u32[]{:S(2)}) collective-permute-start(bf16[8,1024]{1,0:T(8,128)(2,1)S(1)} %fusion.213), channel_id=1, source_target_pairs={{8,0},{16,8},{24,16},{32,24},{40,32},{48,40},{56,48},{64,56},{72,6... | collective-permute-start | bytes 49160 | tf_op jit(solution)/shard_map/while/body/eval_jaxpr/ppermute | solution.py:22
  685.3 7.7 %collective-permute-start.1 = (bf16[8,1024]{1,0:T(8,128)(2,1)S(1)}, bf16[8,1024]{1,0:T(8,128)(2,1)S(1)}, u32[]{:S(2)}, u32[]{:S(2)}) collective-permute-start(bf16[8,1024]{1,0:T(8,128)(2,1)S(1)} %fusion.213), channel_id=1, source_target_pairs={{8,0},{16,8},{24,16},{32,24},{40,32},{48,40},{56,48},{64,56},{72,6... | collective-permute-start | bytes 49160 | tf_op jit(solution)/shard_map/while/body/eval_jaxpr/ppermute | solution.py:22
  693.1 7.7 %collective-permute-start.1 = (bf16[8,1024]{1,0:T(8,128)(2,1)S(1)}, bf16[8,1024]{1,0:T(8,128)(2,1)S(1)}, u32[]{:S(2)}, u32[]{:S(2)}) collective-permute-start(bf16[8,1024]{1,0:T(8,128)(2,1)S(1)} %fusion.213), channel_id=1, source_target_pairs={{8,0},{16,8},{24,16},{32,24},{40,32},{48,40},{56,48},{64,56},{72,6... | collective-permute-start | bytes 49160 | tf_op jit(solution)/shard_map/while/body/eval_jaxpr/ppermute | solution.py:22
  700.9 7.7 %collective-permute-start.1 = (bf16[8,1024]{1,0:T(8,128)(2,1)S(1)}, bf16[8,1024]{1,0:T(8,128)(2,1)S(1)}, u32[]{:S(2)}, u32[]{:S(2)}) collective-permute-start(bf16[8,1024]{1,0:T(8,128)(2,1)S(1)} %fusion.213), channel_id=1, source_target_pairs={{8,0},{16,8},{24,16},{32,24},{40,32},{48,40},{56,48},{64,56},{72,6... | collective-permute-start | bytes 49160 | tf_op jit(solution)/shard_map/while/body/eval_jaxpr/ppermute | solution.py:22
  708.7 7.7 %collective-permute-start.1 = (bf16[8,1024]{1,0:T(8,128)(2,1)S(1)}, bf16[8,1024]{1,0:T(8,128)(2,1)S(1)}, u32[]{:S(2)}, u32[]{:S(2)}) collective-permute-start(bf16[8,1024]{1,0:T(8,128)(2,1)S(1)} %fusion.213), channel_id=1, source_target_pairs={{8,0},{16,8},{24,16},{32,24},{40,32},{48,40},{56,48},{64,56},{72,6... | collective-permute-start | bytes 49160 | tf_op jit(solution)/shard_map/while/body/eval_jaxpr/ppermute | solution.py:22
  716.5 7.8 %collective-permute-start.1 = (bf16[8,1024]{1,0:T(8,128)(2,1)S(1)}, bf16[8,1024]{1,0:T(8,128)(2,1)S(1)}, u32[]{:S(2)}, u32[]{:S(2)}) collective-permute-start(bf16[8,1024]{1,0:T(8,128)(2,1)S(1)} %fusion.213), channel_id=1, source_target_pairs={{8,0},{16,8},{24,16},{32,24},{40,32},{48,40},{56,48},{64,56},{72,6... | collective-permute-start | bytes 49160 | tf_op jit(solution)/shard_map/while/body/eval_jaxpr/ppermute | solution.py:22
  724.5 7.7 %collective-permute-start.1 = (bf16[8,1024]{1,0:T(8,128)(2,1)S(1)}, bf16[8,1024]{1,0:T(8,128)(2,1)S(1)}, u32[]{:S(2)}, u32[]{:S(2)}) collective-permute-start(bf16[8,1024]{1,0:T(8,128)(2,1)S(1)} %fusion.213), channel_id=1, source_target_pairs={{8,0},{16,8},{24,16},{32,24},{40,32},{48,40},{56,48},{64,56},{72,6... | collective-permute-start | bytes 49160 | tf_op jit(solution)/shard_map/while/body/eval_jaxpr/ppermute | solution.py:22
  732.3 7.7 %collective-permute-start.1 = (bf16[8,1024]{1,0:T(8,128)(2,1)S(1)}, bf16[8,1024]{1,0:T(8,128)(2,1)S(1)}, u32[]{:S(2)}, u32[]{:S(2)}) collective-permute-start(bf16[8,1024]{1,0:T(8,128)(2,1)S(1)} %fusion.213), channel_id=1, source_target_pairs={{8,0},{16,8},{24,16},{32,24},{40,32},{48,40},{56,48},{64,56},{72,6... | collective-permute-start | bytes 49160 | tf_op jit(solution)/shard_map/while/body/eval_jaxpr/ppermute | solution.py:22
  740.1 7.7 %collective-permute-start.1 = (bf16[8,1024]{1,0:T(8,128)(2,1)S(1)}, bf16[8,1024]{1,0:T(8,128)(2,1)S(1)}, u32[]{:S(2)}, u32[]{:S(2)}) collective-permute-start(bf16[8,1024]{1,0:T(8,128)(2,1)S(1)} %fusion.213), channel_id=1, source_target_pairs={{8,0},{16,8},{24,16},{32,24},{40,32},{48,40},{56,48},{64,56},{72,6... | collective-permute-start | bytes 49160 | tf_op jit(solution)/shard_map/while/body/eval_jaxpr/ppermute | solution.py:22
  (43 other events, 177.7 us)
Sparse Core Ops, SparseCore 0:
  11.1 38.1 all-gather.7
  261.2 70.5 all-gather.11
  334.0 70.3 all-gather.9
  426.3 28.7 all-reduce.2
  480.3 86.8 reduce-scatter.1
  568.8 31.9 all-gather.13
